TPU v7x, 512 devices: a whole 4x4x16 slice. The times are simulated.
512 devices in a mesh: pipe: 16 (over z), seq: 8 (over y, core), dp: 4 (over x).
Axes of the slice: x: 4, y: 4, z: 16, core: 2. Of those that a mesh axis runs over, the one named last changes fastest.
Arguments:
- acts: bfloat16 [16, 4, 1024, 8192], P('pipe', 'dp', 'seq'), may hold values from -6 to 6
- top_grad: bfloat16 [4, 1024, 8192], P('dp', 'seq'), may hold values from -6 to 6
- a_rows: bfloat16 [16, 32, 8192], P('pipe', None, ('seq', 'dp')), may hold values from -1 to 1
- b_rows: bfloat16 [16, 32, 8192], P('pipe', None, ('seq', 'dp')), may hold values from -0.375 to 0.375
- gain: bfloat16 [16, 8192], P('pipe', ('seq', 'dp')), may hold values from 0.5 to 1.5
Outputs:
- grad_a: float32 [16, 32, 8192], P('pipe', None, ('seq', 'dp'))
- grad_b: float32 [16, 32, 8192], P('pipe', None, ('seq', 'dp'))
- grad_gain: float32 [16, 8192], P('pipe', ('seq', 'dp'))
- clip_factors: float32 [4], P('dp')
All inputs are finite; a program needn't handle non-finite values.
Results may differ from a plain program's by a relative error of at most 0.019.
Values may be sent and summed in bfloat16 or wider, within the bound.
No kernel may reach another device: no remote copies, remote signals or barrier semaphores. Data moves between devices by JAX's collectives and lax.ppermute only.
A program may use at most 64 MiB of HBM per device.

v0:
```python
import math
import jax
import jax.numpy as jnp
from jax import lax
from jax.sharding import PartitionSpec as P

rows_per_block = 32


def from_behind(value, axis, steps):
    count = lax.axis_size(axis)
    initial, last = (max(0, -steps), min(count, count - steps))
    return lax.ppermute(value, axis, [(source, source + steps) for source in range(initial, last)])


def on_device(acts, top_grad, a_rows, b_rows, gain):
    sections = lax.axis_size("pipe")
    section = lax.axis_index("pipe")
    hidden = acts[0, 0]
    top = top_grad[0]
    a_whole, b_whole, gain_whole = (
        lax.all_gather(a_rows, ("seq", "dp"), axis=2, tiled=True),
        lax.all_gather(b_rows, ("seq", "dp"), axis=2, tiled=True),
        lax.all_gather(gain[:, None, :], ("seq", "dp"), axis=2, tiled=True),
    )
    a_full = a_whole[0]
    b_full = b_whole[0]
    gain_float = gain_whole[0, 0].astype(jnp.float32)
    rows, width = hidden.shape
    rank = a_full.shape[0]
    block_total = rows // rows_per_block
    hidden_float = hidden.astype(jnp.float32)
    inverse_root_mean = jnp.sqrt(
        jnp.mean(hidden_float * hidden_float, axis=-1, keepdims=True) + 1e-05
    )
    input_normalized = hidden_float / inverse_root_mean
    normalized_rows = (input_normalized * gain_float).astype(jnp.bfloat16)
    low = jnp.dot(normalized_rows, a_full.T, preferred_element_type=jnp.float32).astype(
        jnp.bfloat16
    )
    contract_last = (((1,), (1,)), ((), ()))
    contract_first = (((0,), (0,)), ((), ()))

    def back_block(upstream_gradient, block_offset):
        input_portion = lax.dynamic_slice_in_dim(input_normalized, block_offset, rows_per_block, 0)
        r_part = lax.dynamic_slice_in_dim(inverse_root_mean, block_offset, rows_per_block, 0)
        d_low = lax.dot_general(
            upstream_gradient, b_full, contract_last, preferred_element_type=jnp.float32
        ).astype(jnp.bfloat16)
        normalized_gradient = jnp.dot(d_low, a_full, preferred_element_type=jnp.float32)
        input_gradient = normalized_gradient * gain_float
        hidden_gradient = (
            upstream_gradient.astype(jnp.float32)
            + (
                input_gradient
                - input_portion * jnp.mean(input_gradient * input_portion, axis=-1, keepdims=True)
            )
            / r_part
        )
        return hidden_gradient.astype(jnp.bfloat16)

    def turn(turn_index, carry):
        incoming, mine = carry
        block_index = turn_index - (sections - 1 - section)
        inside = jnp.logical_and(block_index >= 0, block_index < block_total)
        block_offset = jnp.clip(block_index, 0, block_total - 1) * rows_per_block
        top_block = lax.dynamic_slice_in_dim(top, block_offset, rows_per_block, 0)
        source = jnp.where(section == sections - 1, top_block, incoming)
        kept = lax.dynamic_slice_in_dim(mine, block_offset, rows_per_block, 0)
        mine = lax.dynamic_update_slice_in_dim(
            mine, jnp.where(inside, source, kept), block_offset, 0
        )
        result = back_block(source, block_offset)
        incoming = from_behind(result, "pipe", -1)
        return (incoming, mine)

    begin = (
        jnp.zeros((rows_per_block, width), jnp.bfloat16),
        jnp.zeros((rows, width), jnp.bfloat16),
    )
    mine = lax.fori_loop(0, sections + block_total - 1, turn, begin)[1]
    d_low = lax.dot_general(mine, b_full, contract_last, preferred_element_type=jnp.float32).astype(
        jnp.bfloat16
    )
    normalized_gradient = jnp.dot(d_low, a_full, preferred_element_type=jnp.float32)
    grad_a = lax.dot_general(
        d_low, normalized_rows, contract_first, preferred_element_type=jnp.float32
    )
    grad_b = lax.dot_general(low, mine, contract_first, preferred_element_type=jnp.float32)
    gain_gradient = jnp.sum(normalized_gradient * input_normalized, axis=0)[None, :]
    grad_a, grad_b, gain_gradient = (grad_a, grad_b, gain_gradient)
    sum_a, sum_b, sum_g = lax.psum((grad_a, grad_b, gain_gradient), "seq")
    square = jnp.sum(sum_a * sum_a) + jnp.sum(sum_b * sum_b) + jnp.sum(sum_g * sum_g)
    total = lax.psum(square, "pipe")
    share = width // lax.axis_size("seq")
    offset = lax.axis_index("seq") * share
    part_a = lax.dynamic_slice_in_dim(sum_a, offset, share, 1)
    part_b = lax.dynamic_slice_in_dim(sum_b, offset, share, 1)
    part_g = lax.dynamic_slice_in_dim(sum_g, offset, share, 1)
    bound = math.sqrt(sections * (2 * rank + 1) * width)
    factor = bound / (jnp.sqrt(total) + 0.01 * bound)
    out_a, out_b, out_g = (
        lax.psum_scatter(factor * part_a, "dp", scatter_dimension=1, tiled=True),
        lax.psum_scatter(factor * part_b, "dp", scatter_dimension=1, tiled=True),
        lax.psum_scatter(factor * part_g, "dp", scatter_dimension=1, tiled=True),
    )
    return (out_a[None], out_b[None], out_g, jnp.reshape(factor, (1,)))


def solution(mesh):
    in_specs = (
        P("pipe", "dp", "seq", None),
        P("dp", "seq", None),
        P("pipe", None, ("seq", "dp")),
        P("pipe", None, ("seq", "dp")),
        P("pipe", ("seq", "dp")),
    )
    out_specs = (
        P("pipe", None, ("seq", "dp")),
        P("pipe", None, ("seq", "dp")),
        P("pipe", ("seq", "dp")),
        P("dp"),
    )
    return jax.shard_map(
        on_device, mesh=mesh, in_specs=in_specs, out_specs=out_specs, check_vma=False
    )
```

profile of v0, /device:TPU:8, one launch (start us, length us, event | category | flops | bytes accessed | tf_op | source)
XLA Modules:
  0.0 737.9 jit_solution(11694105464308485738)
XLA Ops:
  9.5 2.4 fusion.1
  11.9 35.9 %all_gather.10 = bf16[1,32,8192]{2,1,0:T(8,128)(2,1)S(1)} all-gather(bf16[1,32,256]{2,1,0:T(8,128)(2,1)S(1)} %copy-done.2), channel_id=1, replica_groups=mesh['pipe'=16,'seq'=8,'dp'=4] {'seq','dp'}, dimensions={2}, use_global_device_ids=true | all-gather | bytes 540672 | tf_op jit(solution)/shard_map/all_gather | solution.py:22
  47.8 34.2 %all-gather = bf16[1,8192]{1,0:T(2,128)(2,1)S(1)} all-gather(bf16[1,256]{1,0:T(2,128)(2,1)S(1)} %copy-done.4), channel_id=2, replica_groups=mesh['pipe'=16,'seq'=8,'dp'=4] {'seq','dp'}, dimensions={1}, use_global_device_ids=true | all-gather | bytes 16896 | tf_op jit(solution)/shard_map/all_gather | solution.py:24
  82.1 32.9 %all_gather.9 = bf16[1,32,8192]{2,1,0:T(8,128)(2,1)S(1)} all-gather(bf16[1,32,256]{2,1,0:T(8,128)(2,1)S(1)} %copy-done.3), channel_id=1, replica_groups=mesh['pipe'=16,'seq'=8,'dp'=4] {'seq','dp'}, dimensions={2}, use_global_device_ids=true | all-gather | bytes 540672 | tf_op jit(solution)/shard_map/all_gather | solution.py:23
  116.6 392.1 %while.17 = (s32[]{:T(128)}, bf16[32,8192]{1,0:T(8,128)(2,1)S(1)}, bf16[128,8192]{1,0:T(8,128)(2,1)}, pred[]{:T(512)}, s32[]{:T(128)}, /*index=5*/bf16[128,8192]...) while((s32[]{:T(128)}, bf16[32,8192]{1,0:T(8,128)(2,1)S(1)}, ...), condition=%wide.region_3.4_spmd, body=%wide.region_1.3_spmd.sunk | while | flops 36439052 | bytes 11568829 | solution.py:81
  121.0 2.3 add_convert_fusion.2
  124.6 14.6 %collective-permute-done = bf16[32,8192]{1,0:T(8,128)(2,1)S(1)} collective-permute-done((bf16[32,8192]{1,0:T(8,128)(2,1)}, bf16[32,8192]{1,0:T(8,128)(2,1)S(1)}, u32[]{:S(2)}, u32[]{:S(2)}) %collective-permute-start) | collective-permute-done | bytes 524320 | tf_op jit(solution)/shard_map/while/body/eval_jaxpr/ppermute | solution.py:13
  143.6 2.3 add_convert_fusion.2
  147.2 13.7 %collective-permute-done = bf16[32,8192]{1,0:T(8,128)(2,1)S(1)} collective-permute-done((bf16[32,8192]{1,0:T(8,128)(2,1)}, bf16[32,8192]{1,0:T(8,128)(2,1)S(1)}, u32[]{:S(2)}, u32[]{:S(2)}) %collective-permute-start) | collective-permute-done | bytes 524320 | tf_op jit(solution)/shard_map/while/body/eval_jaxpr/ppermute | solution.py:13
  165.3 2.3 add_convert_fusion.2
  168.9 12.9 %collective-permute-done = bf16[32,8192]{1,0:T(8,128)(2,1)S(1)} collective-permute-done((bf16[32,8192]{1,0:T(8,128)(2,1)}, bf16[32,8192]{1,0:T(8,128)(2,1)S(1)}, u32[]{:S(2)}, u32[]{:S(2)}) %collective-permute-start) | collective-permute-done | bytes 524320 | tf_op jit(solution)/shard_map/while/body/eval_jaxpr/ppermute | solution.py:13
  186.2 2.3 add_convert_fusion.2
  189.7 12.0 %collective-permute-done = bf16[32,8192]{1,0:T(8,128)(2,1)S(1)} collective-permute-done((bf16[32,8192]{1,0:T(8,128)(2,1)}, bf16[32,8192]{1,0:T(8,128)(2,1)S(1)}, u32[]{:S(2)}, u32[]{:S(2)}) %collective-permute-start) | collective-permute-done | bytes 524320 | tf_op jit(solution)/shard_map/while/body/eval_jaxpr/ppermute | solution.py:13
  206.2 2.3 add_convert_fusion.2
  209.8 12.6 %collective-permute-done = bf16[32,8192]{1,0:T(8,128)(2,1)S(1)} collective-permute-done((bf16[32,8192]{1,0:T(8,128)(2,1)}, bf16[32,8192]{1,0:T(8,128)(2,1)S(1)}, u32[]{:S(2)}, u32[]{:S(2)}) %collective-permute-start) | collective-permute-done | bytes 524320 | tf_op jit(solution)/shard_map/while/body/eval_jaxpr/ppermute | solution.py:13
  226.7 2.3 add_convert_fusion.2
  230.3 11.7 %collective-permute-done = bf16[32,8192]{1,0:T(8,128)(2,1)S(1)} collective-permute-done((bf16[32,8192]{1,0:T(8,128)(2,1)}, bf16[32,8192]{1,0:T(8,128)(2,1)S(1)}, u32[]{:S(2)}, u32[]{:S(2)}) %collective-permute-start) | collective-permute-done | bytes 524320 | tf_op jit(solution)/shard_map/while/body/eval_jaxpr/ppermute | solution.py:13
  246.4 2.3 add_convert_fusion.2
  250.0 10.8 %collective-permute-done = bf16[32,8192]{1,0:T(8,128)(2,1)S(1)} collective-permute-done((bf16[32,8192]{1,0:T(8,128)(2,1)}, bf16[32,8192]{1,0:T(8,128)(2,1)S(1)}, u32[]{:S(2)}, u32[]{:S(2)}) %collective-permute-start) | collective-permute-done | bytes 524320 | tf_op jit(solution)/shard_map/while/body/eval_jaxpr/ppermute | solution.py:13
  265.2 2.3 add_convert_fusion.2
  268.8 10.4 %collective-permute-done = bf16[32,8192]{1,0:T(8,128)(2,1)S(1)} collective-permute-done((bf16[32,8192]{1,0:T(8,128)(2,1)}, bf16[32,8192]{1,0:T(8,128)(2,1)S(1)}, u32[]{:S(2)}, u32[]{:S(2)}) %collective-permute-start) | collective-permute-done | bytes 524320 | tf_op jit(solution)/shard_map/while/body/eval_jaxpr/ppermute | solution.py:13
  287.2 10.7 %collective-permute-done = bf16[32,8192]{1,0:T(8,128)(2,1)S(1)} collective-permute-done((bf16[32,8192]{1,0:T(8,128)(2,1)}, bf16[32,8192]{1,0:T(8,128)(2,1)S(1)}, u32[]{:S(2)}, u32[]{:S(2)}) %collective-permute-start) | collective-permute-done | bytes 524320 | tf_op jit(solution)/shard_map/while/body/eval_jaxpr/ppermute | solution.py:13
  302.3 2.3 add_convert_fusion.2
  305.9 11.2 %collective-permute-done = bf16[32,8192]{1,0:T(8,128)(2,1)S(1)} collective-permute-done((bf16[32,8192]{1,0:T(8,128)(2,1)}, bf16[32,8192]{1,0:T(8,128)(2,1)S(1)}, u32[]{:S(2)}, u32[]{:S(2)}) %collective-permute-start) | collective-permute-done | bytes 524320 | tf_op jit(solution)/shard_map/while/body/eval_jaxpr/ppermute | solution.py:13
  321.5 2.3 add_convert_fusion.2
  325.0 11.2 %collective-permute-done = bf16[32,8192]{1,0:T(8,128)(2,1)S(1)} collective-permute-done((bf16[32,8192]{1,0:T(8,128)(2,1)}, bf16[32,8192]{1,0:T(8,128)(2,1)S(1)}, u32[]{:S(2)}, u32[]{:S(2)}) %collective-permute-start) | collective-permute-done | bytes 524320 | tf_op jit(solution)/shard_map/while/body/eval_jaxpr/ppermute | solution.py:13
  340.6 2.3 add_convert_fusion.2
  344.2 11.2 %collective-permute-done = bf16[32,8192]{1,0:T(8,128)(2,1)S(1)} collective-permute-done((bf16[32,8192]{1,0:T(8,128)(2,1)}, bf16[32,8192]{1,0:T(8,128)(2,1)S(1)}, u32[]{:S(2)}, u32[]{:S(2)}) %collective-permute-start) | collective-permute-done | bytes 524320 | tf_op jit(solution)/shard_map/while/body/eval_jaxpr/ppermute | solution.py:13
  359.8 2.3 add_convert_fusion.2
  363.4 11.2 %collective-permute-done = bf16[32,8192]{1,0:T(8,128)(2,1)S(1)} collective-permute-done((bf16[32,8192]{1,0:T(8,128)(2,1)}, bf16[32,8192]{1,0:T(8,128)(2,1)S(1)}, u32[]{:S(2)}, u32[]{:S(2)}) %collective-permute-start) | collective-permute-done | bytes 524320 | tf_op jit(solution)/shard_map/while/body/eval_jaxpr/ppermute | solution.py:13
  379.0 2.3 add_convert_fusion.2
  382.6 11.9 %collective-permute-done = bf16[32,8192]{1,0:T(8,128)(2,1)S(1)} collective-permute-done((bf16[32,8192]{1,0:T(8,128)(2,1)}, bf16[32,8192]{1,0:T(8,128)(2,1)S(1)}, u32[]{:S(2)}, u32[]{:S(2)}) %collective-permute-start) | collective-permute-done | bytes 524320 | tf_op jit(solution)/shard_map/while/body/eval_jaxpr/ppermute | solution.py:13
  398.9 2.3 add_convert_fusion.2
  402.5 13.4 %collective-permute-done = bf16[32,8192]{1,0:T(8,128)(2,1)S(1)} collective-permute-done((bf16[32,8192]{1,0:T(8,128)(2,1)}, bf16[32,8192]{1,0:T(8,128)(2,1)S(1)}, u32[]{:S(2)}, u32[]{:S(2)}) %collective-permute-start) | collective-permute-done | bytes 524320 | tf_op jit(solution)/shard_map/while/body/eval_jaxpr/ppermute | solution.py:13
  423.9 15.3 %collective-permute-done = bf16[32,8192]{1,0:T(8,128)(2,1)S(1)} collective-permute-done((bf16[32,8192]{1,0:T(8,128)(2,1)}, bf16[32,8192]{1,0:T(8,128)(2,1)S(1)}, u32[]{:S(2)}, u32[]{:S(2)}) %collective-permute-start) | collective-permute-done | bytes 524320 | tf_op jit(solution)/shard_map/while/body/eval_jaxpr/ppermute | solution.py:13
  447.2 16.1 %collective-permute-done = bf16[32,8192]{1,0:T(8,128)(2,1)S(1)} collective-permute-done((bf16[32,8192]{1,0:T(8,128)(2,1)}, bf16[32,8192]{1,0:T(8,128)(2,1)S(1)}, u32[]{:S(2)}, u32[]{:S(2)}) %collective-permute-start) | collective-permute-done | bytes 524320 | tf_op jit(solution)/shard_map/while/body/eval_jaxpr/ppermute | solution.py:13
  471.3 17.4 %collective-permute-done = bf16[32,8192]{1,0:T(8,128)(2,1)S(1)} collective-permute-done((bf16[32,8192]{1,0:T(8,128)(2,1)}, bf16[32,8192]{1,0:T(8,128)(2,1)S(1)}, u32[]{:S(2)}, u32[]{:S(2)}) %collective-permute-start) | collective-permute-done | bytes 524320 | tf_op jit(solution)/shard_map/while/body/eval_jaxpr/ppermute | solution.py:13
  496.7 12.0 %collective-permute-done = bf16[32,8192]{1,0:T(8,128)(2,1)S(1)} collective-permute-done((bf16[32,8192]{1,0:T(8,128)(2,1)}, bf16[32,8192]{1,0:T(8,128)(2,1)S(1)}, u32[]{:S(2)}, u32[]{:S(2)}) %collective-permute-start) | collective-permute-done | bytes 524320 | tf_op jit(solution)/shard_map/while/body/eval_jaxpr/ppermute | solution.py:13
  508.7 4.9 fusion.16
  513.6 2.5 convolution_convert_fusion.1
  518.1 2.4 fusion.11
  520.5 23.2 %psum.30 = f32[1,8192]{1,0:T(1,128)S(1)} all-reduce(f32[1,8192]{1,0:T(1,128)S(1)} %bitcast.65), channel_id=1, replica_groups=mesh['pipe'=16,'seq'=8,'dp'=4] {'seq'}, use_global_device_ids=true, to_apply=%region_9.10 | all-reduce | flops 8192 | bytes 65536 | tf_op jit(solution)/shard_map/psum | solution.py:92
  544.4 57.9 %all-reduce.3.cloned.1.call-done = (f32[32,8192]{1,0:T(8,128)}, f32[32,8192]{1,0:T(8,128)}) async-done(((f32[32,8192]{1,0:T(8,128)}, f32[32,8192]{1,0:T(8,128)}), (f32[32,8192]{1,0:T(8,128)}, f32[32,8192]{1,0:T(8,128)})) %all-reduce.3.cloned.1.call-update) | async-done | bytes 2097168 | tf_op jit(solution)/shard_map/psum | solution.py:92
  602.3 2.4 multiply_reduce_fusion.1
  606.7 31.8 %psum.31 = f32[]{:T(128)} all-reduce(f32[]{:T(128)S(6)} %add.88), channel_id=1, replica_groups=mesh['pipe'=16,'seq'=8,'dp'=4] {'pipe'}, use_global_device_ids=true, to_apply=%region_11.12 | all-reduce | flops 1 | bytes 8 | tf_op jit(solution)/shard_map/psum | solution.py:94
  643.5 23.8 %reduce-scatter.10.cloned.1.call-done = f32[256,1]{1,0:T(8,128)} async-done(((f32[1024,1]{1,0:T(8,128)}), f32[256,1]{1,0:T(8,128)}) %reduce-scatter.10.cloned.1.call-update) | async-done | bytes 1040
  668.9 30.0 %reduce-scatter.8.cloned.1.call-done = f32[32,256]{1,0:T(8,128)} async-done(((f32[32,1024]{1,0:T(8,128)}), f32[32,256]{1,0:T(8,128)}) %reduce-scatter.8.cloned.1.call-update) | async-done | bytes 32784 | tf_op jit(solution)/shard_map/reduce_scatter | solution.py:104
  698.9 31.4 %reduce-scatter.6.cloned.1.call-done = f32[32,256]{1,0:T(8,128)} async-done(((f32[32,1024]{1,0:T(8,128)}), f32[32,256]{1,0:T(8,128)}) %reduce-scatter.6.cloned.1.call-update) | async-done | bytes 32784 | tf_op jit(solution)/shard_map/reduce_scatter | solution.py:103
  (130 shorter events, 131.7 us)
Async XLA Ops:
  7.2 595.1 %all-reduce.3.cloned.1.call-start = ((), (), s32[]{:S(2)}) async-start(), calls=%async_computation.6 | async-start | bytes 4194304 | tf_op jit(solution)/shard_map/psum | solution.py:92
  7.2 2.3 copy-start
  9.5 2.4 copy-start.2
  9.5 38.4 %copy-start.4 = (bf16[1,256]{1,0:T(2,128)(2,1)S(1)}, bf16[1,256]{1,0:T(2,128)(2,1)}, u32[]{:S(2)}) copy-start(bf16[1,256]{1,0:T(2,128)(2,1)} %param.11) | copy-start | bytes 1540
  9.5 72.6 %copy-start.3 = (bf16[1,32,256]{2,1,0:T(8,128)(2,1)S(1)}, bf16[1,32,256]{2,1,0:T(8,128)(2,1)}, u32[]{:S(2)}) copy-start(bf16[1,32,256]{2,1,0:T(8,128)(2,1)} %param.10) | copy-start | bytes 49156
  123.3 15.9 %collective-permute-start = (bf16[32,8192]{1,0:T(8,128)(2,1)}, bf16[32,8192]{1,0:T(8,128)(2,1)S(1)}, u32[]{:S(2)}, u32[]{:S(2)}) collective-permute-start(bf16[32,8192]{1,0:T(8,128)(2,1)} %add_convert_fusion.2), channel_id=1, source_target_pairs={{32,0},{64,32},{96,64},{128,96},{160,128},{192,160},{224,192},{256... | collective-permute-start | bytes 1572872 | tf_op jit(solution)/shard_map/while/body/eval_jaxpr/ppermute | solution.py:13
  145.9 15.0 %collective-permute-start = (bf16[32,8192]{1,0:T(8,128)(2,1)}, bf16[32,8192]{1,0:T(8,128)(2,1)S(1)}, u32[]{:S(2)}, u32[]{:S(2)}) collective-permute-start(bf16[32,8192]{1,0:T(8,128)(2,1)} %add_convert_fusion.2), channel_id=1, source_target_pairs={{32,0},{64,32},{96,64},{128,96},{160,128},{192,160},{224,192},{256... | collective-permute-start | bytes 1572872 | tf_op jit(solution)/shard_map/while/body/eval_jaxpr/ppermute | solution.py:13
  167.6 14.2 %collective-permute-start = (bf16[32,8192]{1,0:T(8,128)(2,1)}, bf16[32,8192]{1,0:T(8,128)(2,1)S(1)}, u32[]{:S(2)}, u32[]{:S(2)}) collective-permute-start(bf16[32,8192]{1,0:T(8,128)(2,1)} %add_convert_fusion.2), channel_id=1, source_target_pairs={{32,0},{64,32},{96,64},{128,96},{160,128},{192,160},{224,192},{256... | collective-permute-start | bytes 1572872 | tf_op jit(solution)/shard_map/while/body/eval_jaxpr/ppermute | solution.py:13
  188.5 13.3 %collective-permute-start = (bf16[32,8192]{1,0:T(8,128)(2,1)}, bf16[32,8192]{1,0:T(8,128)(2,1)S(1)}, u32[]{:S(2)}, u32[]{:S(2)}) collective-permute-start(bf16[32,8192]{1,0:T(8,128)(2,1)} %add_convert_fusion.2), channel_id=1, source_target_pairs={{32,0},{64,32},{96,64},{128,96},{160,128},{192,160},{224,192},{256... | collective-permute-start | bytes 1572872 | tf_op jit(solution)/shard_map/while/body/eval_jaxpr/ppermute | solution.py:13
  208.5 13.8 %collective-permute-start = (bf16[32,8192]{1,0:T(8,128)(2,1)}, bf16[32,8192]{1,0:T(8,128)(2,1)S(1)}, u32[]{:S(2)}, u32[]{:S(2)}) collective-permute-start(bf16[32,8192]{1,0:T(8,128)(2,1)} %add_convert_fusion.2), channel_id=1, source_target_pairs={{32,0},{64,32},{96,64},{128,96},{160,128},{192,160},{224,192},{256... | collective-permute-start | bytes 1572872 | tf_op jit(solution)/shard_map/while/body/eval_jaxpr/ppermute | solution.py:13
  229.0 13.0 %collective-permute-start = (bf16[32,8192]{1,0:T(8,128)(2,1)}, bf16[32,8192]{1,0:T(8,128)(2,1)S(1)}, u32[]{:S(2)}, u32[]{:S(2)}) collective-permute-start(bf16[32,8192]{1,0:T(8,128)(2,1)} %add_convert_fusion.2), channel_id=1, source_target_pairs={{32,0},{64,32},{96,64},{128,96},{160,128},{192,160},{224,192},{256... | collective-permute-start | bytes 1572872 | tf_op jit(solution)/shard_map/while/body/eval_jaxpr/ppermute | solution.py:13
  248.7 12.1 %collective-permute-start = (bf16[32,8192]{1,0:T(8,128)(2,1)}, bf16[32,8192]{1,0:T(8,128)(2,1)S(1)}, u32[]{:S(2)}, u32[]{:S(2)}) collective-permute-start(bf16[32,8192]{1,0:T(8,128)(2,1)} %add_convert_fusion.2), channel_id=1, source_target_pairs={{32,0},{64,32},{96,64},{128,96},{160,128},{192,160},{224,192},{256... | collective-permute-start | bytes 1572872 | tf_op jit(solution)/shard_map/while/body/eval_jaxpr/ppermute | solution.py:13
  267.5 11.6 %collective-permute-start = (bf16[32,8192]{1,0:T(8,128)(2,1)}, bf16[32,8192]{1,0:T(8,128)(2,1)S(1)}, u32[]{:S(2)}, u32[]{:S(2)}) collective-permute-start(bf16[32,8192]{1,0:T(8,128)(2,1)} %add_convert_fusion.2), channel_id=1, source_target_pairs={{32,0},{64,32},{96,64},{128,96},{160,128},{192,160},{224,192},{256... | collective-permute-start | bytes 1572872 | tf_op jit(solution)/shard_map/while/body/eval_jaxpr/ppermute | solution.py:13
  285.9 12.0 %collective-permute-start = (bf16[32,8192]{1,0:T(8,128)(2,1)}, bf16[32,8192]{1,0:T(8,128)(2,1)S(1)}, u32[]{:S(2)}, u32[]{:S(2)}) collective-permute-start(bf16[32,8192]{1,0:T(8,128)(2,1)} %add_convert_fusion.2), channel_id=1, source_target_pairs={{32,0},{64,32},{96,64},{128,96},{160,128},{192,160},{224,192},{256... | collective-permute-start | bytes 1572872 | tf_op jit(solution)/shard_map/while/body/eval_jaxpr/ppermute | solution.py:13
  304.6 12.5 %collective-permute-start = (bf16[32,8192]{1,0:T(8,128)(2,1)}, bf16[32,8192]{1,0:T(8,128)(2,1)S(1)}, u32[]{:S(2)}, u32[]{:S(2)}) collective-permute-start(bf16[32,8192]{1,0:T(8,128)(2,1)} %add_convert_fusion.2), channel_id=1, source_target_pairs={{32,0},{64,32},{96,64},{128,96},{160,128},{192,160},{224,192},{256... | collective-permute-start | bytes 1572872 | tf_op jit(solution)/shard_map/while/body/eval_jaxpr/ppermute | solution.py:13
  323.7 12.5 %collective-permute-start = (bf16[32,8192]{1,0:T(8,128)(2,1)}, bf16[32,8192]{1,0:T(8,128)(2,1)S(1)}, u32[]{:S(2)}, u32[]{:S(2)}) collective-permute-start(bf16[32,8192]{1,0:T(8,128)(2,1)} %add_convert_fusion.2), channel_id=1, source_target_pairs={{32,0},{64,32},{96,64},{128,96},{160,128},{192,160},{224,192},{256... | collective-permute-start | bytes 1572872 | tf_op jit(solution)/shard_map/while/body/eval_jaxpr/ppermute | solution.py:13
  342.9 12.5 %collective-permute-start = (bf16[32,8192]{1,0:T(8,128)(2,1)}, bf16[32,8192]{1,0:T(8,128)(2,1)S(1)}, u32[]{:S(2)}, u32[]{:S(2)}) collective-permute-start(bf16[32,8192]{1,0:T(8,128)(2,1)} %add_convert_fusion.2), channel_id=1, source_target_pairs={{32,0},{64,32},{96,64},{128,96},{160,128},{192,160},{224,192},{256... | collective-permute-start | bytes 1572872 | tf_op jit(solution)/shard_map/while/body/eval_jaxpr/ppermute | solution.py:13
  362.1 12.5 %collective-permute-start = (bf16[32,8192]{1,0:T(8,128)(2,1)}, bf16[32,8192]{1,0:T(8,128)(2,1)S(1)}, u32[]{:S(2)}, u32[]{:S(2)}) collective-permute-start(bf16[32,8192]{1,0:T(8,128)(2,1)} %add_convert_fusion.2), channel_id=1, source_target_pairs={{32,0},{64,32},{96,64},{128,96},{160,128},{192,160},{224,192},{256... | collective-permute-start | bytes 1572872 | tf_op jit(solution)/shard_map/while/body/eval_jaxpr/ppermute | solution.py:13
  381.3 13.2 %collective-permute-start = (bf16[32,8192]{1,0:T(8,128)(2,1)}, bf16[32,8192]{1,0:T(8,128)(2,1)S(1)}, u32[]{:S(2)}, u32[]{:S(2)}) collective-permute-start(bf16[32,8192]{1,0:T(8,128)(2,1)} %add_convert_fusion.2), channel_id=1, source_target_pairs={{32,0},{64,32},{96,64},{128,96},{160,128},{192,160},{224,192},{256... | collective-permute-start | bytes 1572872 | tf_op jit(solution)/shard_map/while/body/eval_jaxpr/ppermute | solution.py:13
  401.2 14.7 %collective-permute-start = (bf16[32,8192]{1,0:T(8,128)(2,1)}, bf16[32,8192]{1,0:T(8,128)(2,1)S(1)}, u32[]{:S(2)}, u32[]{:S(2)}) collective-permute-start(bf16[32,8192]{1,0:T(8,128)(2,1)} %add_convert_fusion.2), channel_id=1, source_target_pairs={{32,0},{64,32},{96,64},{128,96},{160,128},{192,160},{224,192},{256... | collective-permute-start | bytes 1572872 | tf_op jit(solution)/shard_map/while/body/eval_jaxpr/ppermute | solution.py:13
  422.6 16.6 %collective-permute-start = (bf16[32,8192]{1,0:T(8,128)(2,1)}, bf16[32,8192]{1,0:T(8,128)(2,1)S(1)}, u32[]{:S(2)}, u32[]{:S(2)}) collective-permute-start(bf16[32,8192]{1,0:T(8,128)(2,1)} %add_convert_fusion.2), channel_id=1, source_target_pairs={{32,0},{64,32},{96,64},{128,96},{160,128},{192,160},{224,192},{256... | collective-permute-start | bytes 1572872 | tf_op jit(solution)/shard_map/while/body/eval_jaxpr/ppermute | solution.py:13
  445.9 17.4 %collective-permute-start = (bf16[32,8192]{1,0:T(8,128)(2,1)}, bf16[32,8192]{1,0:T(8,128)(2,1)S(1)}, u32[]{:S(2)}, u32[]{:S(2)}) collective-permute-start(bf16[32,8192]{1,0:T(8,128)(2,1)} %add_convert_fusion.2), channel_id=1, source_target_pairs={{32,0},{64,32},{96,64},{128,96},{160,128},{192,160},{224,192},{256... | collective-permute-start | bytes 1572872 | tf_op jit(solution)/shard_map/while/body/eval_jaxpr/ppermute | solution.py:13
  470.0 18.7 %collective-permute-start = (bf16[32,8192]{1,0:T(8,128)(2,1)}, bf16[32,8192]{1,0:T(8,128)(2,1)S(1)}, u32[]{:S(2)}, u32[]{:S(2)}) collective-permute-start(bf16[32,8192]{1,0:T(8,128)(2,1)} %add_convert_fusion.2), channel_id=1, source_target_pairs={{32,0},{64,32},{96,64},{128,96},{160,128},{192,160},{224,192},{256... | collective-permute-start | bytes 1572872 | tf_op jit(solution)/shard_map/while/body/eval_jaxpr/ppermute | solution.py:13
  495.4 13.3 %collective-permute-start = (bf16[32,8192]{1,0:T(8,128)(2,1)}, bf16[32,8192]{1,0:T(8,128)(2,1)S(1)}, u32[]{:S(2)}, u32[]{:S(2)}) collective-permute-start(bf16[32,8192]{1,0:T(8,128)(2,1)} %add_convert_fusion.2), channel_id=1, source_target_pairs={{32,0},{64,32},{96,64},{128,96},{160,128},{192,160},{224,192},{256... | collective-permute-start | bytes 1572872 | tf_op jit(solution)/shard_map/while/body/eval_jaxpr/ppermute | solution.py:13
  513.6 2.6 copy-start.1
  518.0 149.3 %reduce-scatter.10.cloned.1.call-start = ((), (), s32[]{:S(2)}) async-start(), calls=%async_computation.5 | async-start | bytes 655360
  640.3 58.6 %reduce-scatter.8.cloned.1.call-start = ((), (), s32[]{:S(2)}) async-start(), calls=%async_computation.4 | async-start | bytes 163840 | tf_op jit(solution)/shard_map/reduce_scatter | solution.py:104
  641.9 88.4 %reduce-scatter.6.cloned.1.call-start = ((), (), s32[]{:S(2)}) async-start(), calls=%async_computation.3 | async-start | bytes 163840 | tf_op jit(solution)/shard_map/reduce_scatter | solution.py:103
Sparse Core Ops, SparseCore 0:
  518.2 84.0 all-reduce.2
  640.4 26.9 reduce-scatter.9
  670.7 28.1 reduce-scatter.7
  702.1 28.1 reduce-scatter.5
where the time goes:
time: 741 us; the launch traced here: 738 us
  waiting for transfers between devices  383 us (52%)
  blocking collectives  158 us (21%)
  other arithmetic  96.6 us (13%)
  matrix products  51.7 us (7%)
  starting transfers between devices  24.5 us (3%)
  between operations  17.7 us (2%)
    ppermute x19, waiting for transfers between devices, from_behind(): lax.ppermute(value, axis, [(source, source + steps) for source in range(i...  240 us
    psum x1, waiting for transfers between devices, on_device(): sum_a, sum_b, sum_g = lax.psum((grad_a, grad_b, gain_gradient), 'seq')  57.9 us
    convert_element_type x19, other arithmetic, back_block(): return hidden_gradient.astype(jnp.bfloat16)  43.6 us
    dynamic_update_slice x19, other arithmetic, turn(): lax.dynamic_update_slice_in_dim(mine, jnp.where(inside, source, kept), bl...  42 us
    dot_general x19, matrix products, back_block(): jnp.dot(d_low, a_full, preferred_element_type=jnp.float32)  40.1 us
    all_gather x1, blocking collectives, on_device(): lax.all_gather(a_rows, ('seq', 'dp'), axis=2, tiled=True)  35.9 us
    all_gather x1, blocking collectives, on_device(): lax.all_gather(gain[:, None, :], ('seq', 'dp'), axis=2, tiled=True)  34.2 us
    all_gather x1, blocking collectives, on_device(): lax.all_gather(b_rows, ('seq', 'dp'), axis=2, tiled=True)  32.9 us
  transfers between devices with their start and end apart: 23, of which 23 were waited for; matrix products, arithmetic and copies ran while one was open for 1% of the time, Pallas kernels for 0%

commit v1 on v0

--- a/solution.py
+++ b/solution.py
@@ -14,12 +14,22 @@
 
 
 def on_device(acts, top_grad, a_rows, b_rows, gain):
+
+    def choose_local_data(xs):
+        found = []
+        for _ in range(lax.axis_size(("seq", "dp"))):
+            found.append(xs)
+        return jnp.concatenate(
+            lax.all_to_all(jnp.stack(found), axis_name=("seq", "dp"), split_axis=0, concat_axis=0),
+            axis=2,
+        )
+
     sections = lax.axis_size("pipe")
     section = lax.axis_index("pipe")
     hidden = acts[0, 0]
     top = top_grad[0]
     a_whole, b_whole, gain_whole = (
-        lax.all_gather(a_rows, ("seq", "dp"), axis=2, tiled=True),
+        choose_local_data(a_rows),
         lax.all_gather(b_rows, ("seq", "dp"), axis=2, tiled=True),
         lax.all_gather(gain[:, None, :], ("seq", "dp"), axis=2, tiled=True),
     )

time: 741 us -> 716 us (0.966)
  blocking collectives: 158 us -> 121 us
  starting transfers between devices: 24.5 us -> 33.9 us
    all_gather x1 -> x0, blocking collectives: 35.9 us -> none  [on_device(): lax.all_gather(a_rows, ('seq', 'dp'), axis=2, tiled=True)]
    all_to_all x0 -> x1, starting transfers between devices: none -> 9.38 us  [choose_local_data(): lax.all_to_all(jnp.stack(found), axis_name=('seq', 'dp'), split_axis=0, c...]
  transfers between devices with their start and end apart: 23 -> 24, of which waited for: 23 -> 23; matrix products, arithmetic and copies ran while one was open for 1% -> 1% of each run, Pallas kernels for 0% -> 0%
where the time goes in v1:
time: 716 us; the launch traced here: 713 us
  waiting for transfers between devices  387 us (54%)
  blocking collectives  121 us (17%)
  other arithmetic  96.4 us (13%)
  matrix products  50.1 us (7%)
  starting transfers between devices  33.9 us (5%)
  between operations  17.7 us (2%)
  local copies, waits for them, and re-layouts  7.39 us (1%)
    ppermute x19, waiting for transfers between devices, from_behind(): lax.ppermute(value, axis, [(source, source + steps) for source in range(i...  242 us
    psum x1, waiting for transfers between devices, on_device(): sum_a, sum_b, sum_g = lax.psum((grad_a, grad_b, gain_gradient), 'seq')  59.6 us
    convert_element_type x19, other arithmetic, back_block(): return hidden_gradient.astype(jnp.bfloat16)  43.6 us
    dynamic_update_slice x19, other arithmetic, turn(): lax.dynamic_update_slice_in_dim(mine, jnp.where(inside, source, kept), bl...  42 us
    dot_general x19, matrix products, back_block(): jnp.dot(d_low, a_full, preferred_element_type=jnp.float32)  40.1 us
    all_gather x1, blocking collectives, on_device(): lax.all_gather(b_rows, ('seq', 'dp'), axis=2, tiled=True)  33.8 us
    all_gather x1, blocking collectives, on_device(): lax.all_gather(gain[:, None, :], ('seq', 'dp'), axis=2, tiled=True)  31.9 us
    psum x1, blocking collectives, on_device(): total = lax.psum(square, 'pipe')  31.8 us
  transfers between devices with their start and end apart: 24, of which 23 were waited for; matrix products, arithmetic and copies ran while one was open for 1% of the time, Pallas kernels for 0%

profile of v1, /device:TPU:8, one launch (start us, length us, event | category | flops | bytes accessed | tf_op | source)
XLA Modules:
  0.0 713.0 jit_solution(4130603648411270454)
XLA Ops:
  8.9 9.4 %all-to-all-start = ((bf16[32,1,32,256]{3,2,1,0:T(8,128)(2,1)}), bf16[32,1,32,256]{3,2,1,0:T(8,128)(2,1)S(1)}, u32[]{:S(2)}, u32[]{:S(2)}) async-start(bf16[32,1,32,256]{3,2,1,0:T(8,128)(2,1)} %stack.2), calls=%async_computation | async-start | bytes 1048576 | tf_op jit(solution)/shard_map/all_to_all | solution.py:23
  20.5 2.4 fusion.1
  22.9 31.9 %all-gather = bf16[1,8192]{1,0:T(2,128)(2,1)S(1)} all-gather(bf16[1,256]{1,0:T(2,128)(2,1)S(1)} %copy-done.3), channel_id=2, replica_groups=mesh['pipe'=16,'seq'=8,'dp'=4] {'seq','dp'}, dimensions={1}, use_global_device_ids=true | all-gather | bytes 16896 | tf_op jit(solution)/shard_map/all_gather | solution.py:34
  54.8 33.8 %all_gather.6 = bf16[1,32,8192]{2,1,0:T(8,128)(2,1)S(1)} all-gather(bf16[1,32,256]{2,1,0:T(8,128)(2,1)S(1)} %copy-done.2), channel_id=1, replica_groups=mesh['pipe'=16,'seq'=8,'dp'=4] {'seq','dp'}, dimensions={2}, use_global_device_ids=true | all-gather | bytes 540672 | tf_op jit(solution)/shard_map/all_gather | solution.py:33
  90.2 393.6 %while.17 = (s32[]{:T(128)}, bf16[32,8192]{1,0:T(8,128)(2,1)S(1)}, bf16[128,8192]{1,0:T(8,128)(2,1)}, pred[]{:T(512)}, s32[]{:T(128)}, /*index=5*/bf16[128,8192]...) while((s32[]{:T(128)}, bf16[32,8192]{1,0:T(8,128)(2,1)S(1)}, ...), condition=%wide.region_3.4_spmd, body=%wide.region_1.3_spmd.sunk | while | flops 36439052 | bytes 11568829 | solution.py:91
  94.7 2.3 add_convert_fusion.2
  98.3 14.6 %collective-permute-done = bf16[32,8192]{1,0:T(8,128)(2,1)S(1)} collective-permute-done((bf16[32,8192]{1,0:T(8,128)(2,1)}, bf16[32,8192]{1,0:T(8,128)(2,1)S(1)}, u32[]{:S(2)}, u32[]{:S(2)}) %collective-permute-start) | collective-permute-done | bytes 524320 | tf_op jit(solution)/shard_map/while/body/eval_jaxpr/ppermute | solution.py:13
  117.3 2.3 add_convert_fusion.2
  120.9 13.7 %collective-permute-done = bf16[32,8192]{1,0:T(8,128)(2,1)S(1)} collective-permute-done((bf16[32,8192]{1,0:T(8,128)(2,1)}, bf16[32,8192]{1,0:T(8,128)(2,1)S(1)}, u32[]{:S(2)}, u32[]{:S(2)}) %collective-permute-start) | collective-permute-done | bytes 524320 | tf_op jit(solution)/shard_map/while/body/eval_jaxpr/ppermute | solution.py:13
  142.6 12.9 %collective-permute-done = bf16[32,8192]{1,0:T(8,128)(2,1)S(1)} collective-permute-done((bf16[32,8192]{1,0:T(8,128)(2,1)}, bf16[32,8192]{1,0:T(8,128)(2,1)S(1)}, u32[]{:S(2)}, u32[]{:S(2)}) %collective-permute-start) | collective-permute-done | bytes 524320 | tf_op jit(solution)/shard_map/while/body/eval_jaxpr/ppermute | solution.py:13
  159.9 2.3 add_convert_fusion.2
  163.4 13.4 %collective-permute-done = bf16[32,8192]{1,0:T(8,128)(2,1)S(1)} collective-permute-done((bf16[32,8192]{1,0:T(8,128)(2,1)}, bf16[32,8192]{1,0:T(8,128)(2,1)S(1)}, u32[]{:S(2)}, u32[]{:S(2)}) %collective-permute-start) | collective-permute-done | bytes 524320 | tf_op jit(solution)/shard_map/while/body/eval_jaxpr/ppermute | solution.py:13
  181.3 2.3 add_convert_fusion.2
  184.9 12.6 %collective-permute-done = bf16[32,8192]{1,0:T(8,128)(2,1)S(1)} collective-permute-done((bf16[32,8192]{1,0:T(8,128)(2,1)}, bf16[32,8192]{1,0:T(8,128)(2,1)S(1)}, u32[]{:S(2)}, u32[]{:S(2)}) %collective-permute-start) | collective-permute-done | bytes 524320 | tf_op jit(solution)/shard_map/while/body/eval_jaxpr/ppermute | solution.py:13
  201.8 2.3 add_convert_fusion.2
  205.4 11.7 %collective-permute-done = bf16[32,8192]{1,0:T(8,128)(2,1)S(1)} collective-permute-done((bf16[32,8192]{1,0:T(8,128)(2,1)}, bf16[32,8192]{1,0:T(8,128)(2,1)S(1)}, u32[]{:S(2)}, u32[]{:S(2)}) %collective-permute-start) | collective-permute-done | bytes 524320 | tf_op jit(solution)/shard_map/while/body/eval_jaxpr/ppermute | solution.py:13
  221.5 2.3 add_convert_fusion.2
  225.1 10.8 %collective-permute-done = bf16[32,8192]{1,0:T(8,128)(2,1)S(1)} collective-permute-done((bf16[32,8192]{1,0:T(8,128)(2,1)}, bf16[32,8192]{1,0:T(8,128)(2,1)S(1)}, u32[]{:S(2)}, u32[]{:S(2)}) %collective-permute-start) | collective-permute-done | bytes 524320 | tf_op jit(solution)/shard_map/while/body/eval_jaxpr/ppermute | solution.py:13
  240.4 2.3 add_convert_fusion.2
  244.0 10.4 %collective-permute-done = bf16[32,8192]{1,0:T(8,128)(2,1)S(1)} collective-permute-done((bf16[32,8192]{1,0:T(8,128)(2,1)}, bf16[32,8192]{1,0:T(8,128)(2,1)S(1)}, u32[]{:S(2)}, u32[]{:S(2)}) %collective-permute-start) | collective-permute-done | bytes 524320 | tf_op jit(solution)/shard_map/while/body/eval_jaxpr/ppermute | solution.py:13
  262.3 10.7 %collective-permute-done = bf16[32,8192]{1,0:T(8,128)(2,1)S(1)} collective-permute-done((bf16[32,8192]{1,0:T(8,128)(2,1)}, bf16[32,8192]{1,0:T(8,128)(2,1)S(1)}, u32[]{:S(2)}, u32[]{:S(2)}) %collective-permute-start) | collective-permute-done | bytes 524320 | tf_op jit(solution)/shard_map/while/body/eval_jaxpr/ppermute | solution.py:13
  277.4 2.3 add_convert_fusion.2
  281.0 11.2 %collective-permute-done = bf16[32,8192]{1,0:T(8,128)(2,1)S(1)} collective-permute-done((bf16[32,8192]{1,0:T(8,128)(2,1)}, bf16[32,8192]{1,0:T(8,128)(2,1)S(1)}, u32[]{:S(2)}, u32[]{:S(2)}) %collective-permute-start) | collective-permute-done | bytes 524320 | tf_op jit(solution)/shard_map/while/body/eval_jaxpr/ppermute | solution.py:13
  296.6 2.3 add_convert_fusion.2
  300.2 11.2 %collective-permute-done = bf16[32,8192]{1,0:T(8,128)(2,1)S(1)} collective-permute-done((bf16[32,8192]{1,0:T(8,128)(2,1)}, bf16[32,8192]{1,0:T(8,128)(2,1)S(1)}, u32[]{:S(2)}, u32[]{:S(2)}) %collective-permute-start) | collective-permute-done | bytes 524320 | tf_op jit(solution)/shard_map/while/body/eval_jaxpr/ppermute | solution.py:13
  315.8 2.3 add_convert_fusion.2
  319.4 11.2 %collective-permute-done = bf16[32,8192]{1,0:T(8,128)(2,1)S(1)} collective-permute-done((bf16[32,8192]{1,0:T(8,128)(2,1)}, bf16[32,8192]{1,0:T(8,128)(2,1)S(1)}, u32[]{:S(2)}, u32[]{:S(2)}) %collective-permute-start) | collective-permute-done | bytes 524320 | tf_op jit(solution)/shard_map/while/body/eval_jaxpr/ppermute | solution.py:13
  334.9 2.3 add_convert_fusion.2
  338.5 11.2 %collective-permute-done = bf16[32,8192]{1,0:T(8,128)(2,1)S(1)} collective-permute-done((bf16[32,8192]{1,0:T(8,128)(2,1)}, bf16[32,8192]{1,0:T(8,128)(2,1)S(1)}, u32[]{:S(2)}, u32[]{:S(2)}) %collective-permute-start) | collective-permute-done | bytes 524320 | tf_op jit(solution)/shard_map/while/body/eval_jaxpr/ppermute | solution.py:13
  354.1 2.3 add_convert_fusion.2
  357.7 11.9 %collective-permute-done = bf16[32,8192]{1,0:T(8,128)(2,1)S(1)} collective-permute-done((bf16[32,8192]{1,0:T(8,128)(2,1)}, bf16[32,8192]{1,0:T(8,128)(2,1)S(1)}, u32[]{:S(2)}, u32[]{:S(2)}) %collective-permute-start) | collective-permute-done | bytes 524320 | tf_op jit(solution)/shard_map/while/body/eval_jaxpr/ppermute | solution.py:13
  374.1 2.3 add_convert_fusion.2
  377.7 13.4 %collective-permute-done = bf16[32,8192]{1,0:T(8,128)(2,1)S(1)} collective-permute-done((bf16[32,8192]{1,0:T(8,128)(2,1)}, bf16[32,8192]{1,0:T(8,128)(2,1)S(1)}, u32[]{:S(2)}, u32[]{:S(2)}) %collective-permute-start) | collective-permute-done | bytes 524320 | tf_op jit(solution)/shard_map/while/body/eval_jaxpr/ppermute | solution.py:13
  395.4 2.3 add_convert_fusion.2
  399.0 15.3 %collective-permute-done = bf16[32,8192]{1,0:T(8,128)(2,1)S(1)} collective-permute-done((bf16[32,8192]{1,0:T(8,128)(2,1)}, bf16[32,8192]{1,0:T(8,128)(2,1)S(1)}, u32[]{:S(2)}, u32[]{:S(2)}) %collective-permute-start) | collective-permute-done | bytes 524320 | tf_op jit(solution)/shard_map/while/body/eval_jaxpr/ppermute | solution.py:13
  418.7 2.3 add_convert_fusion.2
  422.3 16.1 %collective-permute-done = bf16[32,8192]{1,0:T(8,128)(2,1)S(1)} collective-permute-done((bf16[32,8192]{1,0:T(8,128)(2,1)}, bf16[32,8192]{1,0:T(8,128)(2,1)S(1)}, u32[]{:S(2)}, u32[]{:S(2)}) %collective-permute-start) | collective-permute-done | bytes 524320 | tf_op jit(solution)/shard_map/while/body/eval_jaxpr/ppermute | solution.py:13
  446.4 17.4 %collective-permute-done = bf16[32,8192]{1,0:T(8,128)(2,1)S(1)} collective-permute-done((bf16[32,8192]{1,0:T(8,128)(2,1)}, bf16[32,8192]{1,0:T(8,128)(2,1)S(1)}, u32[]{:S(2)}, u32[]{:S(2)}) %collective-permute-start) | collective-permute-done | bytes 524320 | tf_op jit(solution)/shard_map/while/body/eval_jaxpr/ppermute | solution.py:13
  471.8 12.0 %collective-permute-done = bf16[32,8192]{1,0:T(8,128)(2,1)S(1)} collective-permute-done((bf16[32,8192]{1,0:T(8,128)(2,1)}, bf16[32,8192]{1,0:T(8,128)(2,1)S(1)}, u32[]{:S(2)}, u32[]{:S(2)}) %collective-permute-start) | collective-permute-done | bytes 524320 | tf_op jit(solution)/shard_map/while/body/eval_jaxpr/ppermute | solution.py:13
  483.8 4.9 fusion.16
  488.8 2.5 convolution_convert_fusion.1
  494.0 23.1 %psum.30 = f32[1,8192]{1,0:T(1,128)S(1)} all-reduce(f32[1,8192]{1,0:T(1,128)S(1)} %bitcast.67), channel_id=1, replica_groups=mesh['pipe'=16,'seq'=8,'dp'=4] {'seq'}, use_global_device_ids=true, to_apply=%region_9.10 | all-reduce | flops 8192 | bytes 65536 | tf_op jit(solution)/shard_map/psum | solution.py:102
  517.7 59.6 %all-reduce.3.cloned.1.call-done = (f32[32,8192]{1,0:T(8,128)}, f32[32,8192]{1,0:T(8,128)}) async-done(((f32[32,8192]{1,0:T(8,128)}, f32[32,8192]{1,0:T(8,128)}), (f32[32,8192]{1,0:T(8,128)}, f32[32,8192]{1,0:T(8,128)})) %all-reduce.3.cloned.1.call-update) | async-done | bytes 2097168 | tf_op jit(solution)/shard_map/psum | solution.py:102
  577.4 2.4 multiply_reduce_fusion.1
  581.7 31.8 %psum.31 = f32[]{:T(128)} all-reduce(f32[]{:T(128)S(6)} %add.88), channel_id=1, replica_groups=mesh['pipe'=16,'seq'=8,'dp'=4] {'pipe'}, use_global_device_ids=true, to_apply=%region_11.12 | all-reduce | flops 1 | bytes 8 | tf_op jit(solution)/shard_map/psum | solution.py:104
  618.6 23.8 %reduce-scatter.10.cloned.1.call-done = f32[256,1]{1,0:T(8,128)} async-done(((f32[1024,1]{1,0:T(8,128)}), f32[256,1]{1,0:T(8,128)}) %reduce-scatter.10.cloned.1.call-update) | async-done | bytes 1040
  644.0 30.0 %reduce-scatter.8.cloned.1.call-done = f32[32,256]{1,0:T(8,128)} async-done(((f32[32,1024]{1,0:T(8,128)}), f32[32,256]{1,0:T(8,128)}) %reduce-scatter.8.cloned.1.call-update) | async-done | bytes 32784 | tf_op jit(solution)/shard_map/reduce_scatter | solution.py:114
  674.0 31.4 %reduce-scatter.6.cloned.1.call-done = f32[32,256]{1,0:T(8,128)} async-done(((f32[32,1024]{1,0:T(8,128)}), f32[32,256]{1,0:T(8,128)}) %reduce-scatter.6.cloned.1.call-update) | async-done | bytes 32784 | tf_op jit(solution)/shard_map/reduce_scatter | solution.py:113
  (131 shorter events, 131.8 us)
Async XLA Ops:
  7.2 13.3 %copy-start = (bf16[1,1,128,8192]{3,2,1,0:T(8,128)(2,1)S(1)}, bf16[1,1,128,8192]{3,2,1,0:T(8,128)(2,1)}, u32[]{:S(2)}) copy-start(bf16[1,1,128,8192]{3,2,1,0:T(8,128)(2,1)} %param.7) | copy-start | bytes 6291460
  8.9 79.7 %all-to-all-start = ((bf16[32,1,32,256]{3,2,1,0:T(8,128)(2,1)}), bf16[32,1,32,256]{3,2,1,0:T(8,128)(2,1)S(1)}, u32[]{:S(2)}, u32[]{:S(2)}) async-start(bf16[32,1,32,256]{3,2,1,0:T(8,128)(2,1)} %stack.2), calls=%async_computation | async-start | bytes 1048576 | tf_op jit(solution)/shard_map/all_to_all | solution.py:23
  18.3 559.1 %all-reduce.3.cloned.1.call-start = ((), (), s32[]{:S(2)}) async-start(), calls=%async_computation.7 | async-start | bytes 4194304 | tf_op jit(solution)/shard_map/psum | solution.py:102
  20.4 2.4 copy-start.3
  20.4 34.4 %copy-start.2 = (bf16[1,32,256]{2,1,0:T(8,128)(2,1)S(1)}, bf16[1,32,256]{2,1,0:T(8,128)(2,1)}, u32[]{:S(2)}) copy-start(bf16[1,32,256]{2,1,0:T(8,128)(2,1)} %param.10) | copy-start | bytes 49156
  97.0 15.9 %collective-permute-start = (bf16[32,8192]{1,0:T(8,128)(2,1)}, bf16[32,8192]{1,0:T(8,128)(2,1)S(1)}, u32[]{:S(2)}, u32[]{:S(2)}) collective-permute-start(bf16[32,8192]{1,0:T(8,128)(2,1)} %add_convert_fusion.2), channel_id=1, source_target_pairs={{32,0},{64,32},{96,64},{128,96},{160,128},{192,160},{224,192},{256... | collective-permute-start | bytes 1572872 | tf_op jit(solution)/shard_map/while/body/eval_jaxpr/ppermute | solution.py:13
  119.6 15.0 %collective-permute-start = (bf16[32,8192]{1,0:T(8,128)(2,1)}, bf16[32,8192]{1,0:T(8,128)(2,1)S(1)}, u32[]{:S(2)}, u32[]{:S(2)}) collective-permute-start(bf16[32,8192]{1,0:T(8,128)(2,1)} %add_convert_fusion.2), channel_id=1, source_target_pairs={{32,0},{64,32},{96,64},{128,96},{160,128},{192,160},{224,192},{256... | collective-permute-start | bytes 1572872 | tf_op jit(solution)/shard_map/while/body/eval_jaxpr/ppermute | solution.py:13
  141.3 14.2 %collective-permute-start = (bf16[32,8192]{1,0:T(8,128)(2,1)}, bf16[32,8192]{1,0:T(8,128)(2,1)S(1)}, u32[]{:S(2)}, u32[]{:S(2)}) collective-permute-start(bf16[32,8192]{1,0:T(8,128)(2,1)} %add_convert_fusion.2), channel_id=1, source_target_pairs={{32,0},{64,32},{96,64},{128,96},{160,128},{192,160},{224,192},{256... | collective-permute-start | bytes 1572872 | tf_op jit(solution)/shard_map/while/body/eval_jaxpr/ppermute | solution.py:13
  162.2 14.7 %collective-permute-start = (bf16[32,8192]{1,0:T(8,128)(2,1)}, bf16[32,8192]{1,0:T(8,128)(2,1)S(1)}, u32[]{:S(2)}, u32[]{:S(2)}) collective-permute-start(bf16[32,8192]{1,0:T(8,128)(2,1)} %add_convert_fusion.2), channel_id=1, source_target_pairs={{32,0},{64,32},{96,64},{128,96},{160,128},{192,160},{224,192},{256... | collective-permute-start | bytes 1572872 | tf_op jit(solution)/shard_map/while/body/eval_jaxpr/ppermute | solution.py:13
  183.6 13.9 %collective-permute-start = (bf16[32,8192]{1,0:T(8,128)(2,1)}, bf16[32,8192]{1,0:T(8,128)(2,1)S(1)}, u32[]{:S(2)}, u32[]{:S(2)}) collective-permute-start(bf16[32,8192]{1,0:T(8,128)(2,1)} %add_convert_fusion.2), channel_id=1, source_target_pairs={{32,0},{64,32},{96,64},{128,96},{160,128},{192,160},{224,192},{256... | collective-permute-start | bytes 1572872 | tf_op jit(solution)/shard_map/while/body/eval_jaxpr/ppermute | solution.py:13
  204.1 13.0 %collective-permute-start = (bf16[32,8192]{1,0:T(8,128)(2,1)}, bf16[32,8192]{1,0:T(8,128)(2,1)S(1)}, u32[]{:S(2)}, u32[]{:S(2)}) collective-permute-start(bf16[32,8192]{1,0:T(8,128)(2,1)} %add_convert_fusion.2), channel_id=1, source_target_pairs={{32,0},{64,32},{96,64},{128,96},{160,128},{192,160},{224,192},{256... | collective-permute-start | bytes 1572872 | tf_op jit(solution)/shard_map/while/body/eval_jaxpr/ppermute | solution.py:13
  223.8 12.1 %collective-permute-start = (bf16[32,8192]{1,0:T(8,128)(2,1)}, bf16[32,8192]{1,0:T(8,128)(2,1)S(1)}, u32[]{:S(2)}, u32[]{:S(2)}) collective-permute-start(bf16[32,8192]{1,0:T(8,128)(2,1)} %add_convert_fusion.2), channel_id=1, source_target_pairs={{32,0},{64,32},{96,64},{128,96},{160,128},{192,160},{224,192},{256... | collective-permute-start | bytes 1572872 | tf_op jit(solution)/shard_map/while/body/eval_jaxpr/ppermute | solution.py:13
  242.7 11.6 %collective-permute-start = (bf16[32,8192]{1,0:T(8,128)(2,1)}, bf16[32,8192]{1,0:T(8,128)(2,1)S(1)}, u32[]{:S(2)}, u32[]{:S(2)}) collective-permute-start(bf16[32,8192]{1,0:T(8,128)(2,1)} %add_convert_fusion.2), channel_id=1, source_target_pairs={{32,0},{64,32},{96,64},{128,96},{160,128},{192,160},{224,192},{256... | collective-permute-start | bytes 1572872 | tf_op jit(solution)/shard_map/while/body/eval_jaxpr/ppermute | solution.py:13
  261.0 12.0 %collective-permute-start = (bf16[32,8192]{1,0:T(8,128)(2,1)}, bf16[32,8192]{1,0:T(8,128)(2,1)S(1)}, u32[]{:S(2)}, u32[]{:S(2)}) collective-permute-start(bf16[32,8192]{1,0:T(8,128)(2,1)} %add_convert_fusion.2), channel_id=1, source_target_pairs={{32,0},{64,32},{96,64},{128,96},{160,128},{192,160},{224,192},{256... | collective-permute-start | bytes 1572872 | tf_op jit(solution)/shard_map/while/body/eval_jaxpr/ppermute | solution.py:13
  279.7 12.5 %collective-permute-start = (bf16[32,8192]{1,0:T(8,128)(2,1)}, bf16[32,8192]{1,0:T(8,128)(2,1)S(1)}, u32[]{:S(2)}, u32[]{:S(2)}) collective-permute-start(bf16[32,8192]{1,0:T(8,128)(2,1)} %add_convert_fusion.2), channel_id=1, source_target_pairs={{32,0},{64,32},{96,64},{128,96},{160,128},{192,160},{224,192},{256... | collective-permute-start | bytes 1572872 | tf_op jit(solution)/shard_map/while/body/eval_jaxpr/ppermute | solution.py:13
  298.9 12.5 %collective-permute-start = (bf16[32,8192]{1,0:T(8,128)(2,1)}, bf16[32,8192]{1,0:T(8,128)(2,1)S(1)}, u32[]{:S(2)}, u32[]{:S(2)}) collective-permute-start(bf16[32,8192]{1,0:T(8,128)(2,1)} %add_convert_fusion.2), channel_id=1, source_target_pairs={{32,0},{64,32},{96,64},{128,96},{160,128},{192,160},{224,192},{256... | collective-permute-start | bytes 1572872 | tf_op jit(solution)/shard_map/while/body/eval_jaxpr/ppermute | solution.py:13
  318.1 12.5 %collective-permute-start = (bf16[32,8192]{1,0:T(8,128)(2,1)}, bf16[32,8192]{1,0:T(8,128)(2,1)S(1)}, u32[]{:S(2)}, u32[]{:S(2)}) collective-permute-start(bf16[32,8192]{1,0:T(8,128)(2,1)} %add_convert_fusion.2), channel_id=1, source_target_pairs={{32,0},{64,32},{96,64},{128,96},{160,128},{192,160},{224,192},{256... | collective-permute-start | bytes 1572872 | tf_op jit(solution)/shard_map/while/body/eval_jaxpr/ppermute | solution.py:13
  337.2 12.5 %collective-permute-start = (bf16[32,8192]{1,0:T(8,128)(2,1)}, bf16[32,8192]{1,0:T(8,128)(2,1)S(1)}, u32[]{:S(2)}, u32[]{:S(2)}) collective-permute-start(bf16[32,8192]{1,0:T(8,128)(2,1)} %add_convert_fusion.2), channel_id=1, source_target_pairs={{32,0},{64,32},{96,64},{128,96},{160,128},{192,160},{224,192},{256... | collective-permute-start | bytes 1572872 | tf_op jit(solution)/shard_map/while/body/eval_jaxpr/ppermute | solution.py:13
  356.4 13.2 %collective-permute-start = (bf16[32,8192]{1,0:T(8,128)(2,1)}, bf16[32,8192]{1,0:T(8,128)(2,1)S(1)}, u32[]{:S(2)}, u32[]{:S(2)}) collective-permute-start(bf16[32,8192]{1,0:T(8,128)(2,1)} %add_convert_fusion.2), channel_id=1, source_target_pairs={{32,0},{64,32},{96,64},{128,96},{160,128},{192,160},{224,192},{256... | collective-permute-start | bytes 1572872 | tf_op jit(solution)/shard_map/while/body/eval_jaxpr/ppermute | solution.py:13
  376.4 14.7 %collective-permute-start = (bf16[32,8192]{1,0:T(8,128)(2,1)}, bf16[32,8192]{1,0:T(8,128)(2,1)S(1)}, u32[]{:S(2)}, u32[]{:S(2)}) collective-permute-start(bf16[32,8192]{1,0:T(8,128)(2,1)} %add_convert_fusion.2), channel_id=1, source_target_pairs={{32,0},{64,32},{96,64},{128,96},{160,128},{192,160},{224,192},{256... | collective-permute-start | bytes 1572872 | tf_op jit(solution)/shard_map/while/body/eval_jaxpr/ppermute | solution.py:13
  397.7 16.6 %collective-permute-start = (bf16[32,8192]{1,0:T(8,128)(2,1)}, bf16[32,8192]{1,0:T(8,128)(2,1)S(1)}, u32[]{:S(2)}, u32[]{:S(2)}) collective-permute-start(bf16[32,8192]{1,0:T(8,128)(2,1)} %add_convert_fusion.2), channel_id=1, source_target_pairs={{32,0},{64,32},{96,64},{128,96},{160,128},{192,160},{224,192},{256... | collective-permute-start | bytes 1572872 | tf_op jit(solution)/shard_map/while/body/eval_jaxpr/ppermute | solution.py:13
  421.0 17.4 %collective-permute-start = (bf16[32,8192]{1,0:T(8,128)(2,1)}, bf16[32,8192]{1,0:T(8,128)(2,1)S(1)}, u32[]{:S(2)}, u32[]{:S(2)}) collective-permute-start(bf16[32,8192]{1,0:T(8,128)(2,1)} %add_convert_fusion.2), channel_id=1, source_target_pairs={{32,0},{64,32},{96,64},{128,96},{160,128},{192,160},{224,192},{256... | collective-permute-start | bytes 1572872 | tf_op jit(solution)/shard_map/while/body/eval_jaxpr/ppermute | solution.py:13
  445.1 18.7 %collective-permute-start = (bf16[32,8192]{1,0:T(8,128)(2,1)}, bf16[32,8192]{1,0:T(8,128)(2,1)S(1)}, u32[]{:S(2)}, u32[]{:S(2)}) collective-permute-start(bf16[32,8192]{1,0:T(8,128)(2,1)} %add_convert_fusion.2), channel_id=1, source_target_pairs={{32,0},{64,32},{96,64},{128,96},{160,128},{192,160},{224,192},{256... | collective-permute-start | bytes 1572872 | tf_op jit(solution)/shard_map/while/body/eval_jaxpr/ppermute | solution.py:13
  470.5 13.3 %collective-permute-start = (bf16[32,8192]{1,0:T(8,128)(2,1)}, bf16[32,8192]{1,0:T(8,128)(2,1)S(1)}, u32[]{:S(2)}, u32[]{:S(2)}) collective-permute-start(bf16[32,8192]{1,0:T(8,128)(2,1)} %add_convert_fusion.2), channel_id=1, source_target_pairs={{32,0},{64,32},{96,64},{128,96},{160,128},{192,160},{224,192},{256... | collective-permute-start | bytes 1572872 | tf_op jit(solution)/shard_map/while/body/eval_jaxpr/ppermute | solution.py:13
  488.8 2.6 copy-start.1
  493.2 149.3 %reduce-scatter.10.cloned.1.call-start = ((), (), s32[]{:S(2)}) async-start(), calls=%async_computation.6 | async-start | bytes 655360
  615.3 58.6 %reduce-scatter.8.cloned.1.call-start = ((), (), s32[]{:S(2)}) async-start(), calls=%async_computation.5 | async-start | bytes 163840 | tf_op jit(solution)/shard_map/reduce_scatter | solution.py:114
  617.0 88.4 %reduce-scatter.6.cloned.1.call-start = ((), (), s32[]{:S(2)}) async-start(), calls=%async_computation.4 | async-start | bytes 163840 | tf_op jit(solution)/shard_map/reduce_scatter | solution.py:113
Sparse Core Ops, SparseCore 0:
  493.3 84.0 all-reduce.2
  615.5 26.9 reduce-scatter.9
  645.8 28.1 reduce-scatter.7
  677.2 28.1 reduce-scatter.5
